TPU v7x, 512 devices: a whole 4x4x16 slice. The times are simulated.
512 devices in a mesh: req: 32 (over y, x, core), grp: 16 (over z).
Axes of the slice: x: 4, y: 4, z: 16, core: 2. Of those that a mesh axis runs over, the one named last changes fastest.
Arguments:
- normed_token_input: bfloat16 [256, 8192], P(None, 'req'), may hold values from -6 to 6
- key_value_weight: bfloat16 [8192, 2048], P('req', 'grp'), may hold values from -0.0625 to 0.0625
- adapter_down_weight: bfloat16 [8192, 128, 128], P('req', 'grp'), may hold values from -0.0625 to 0.0625
- adapter_up_weight: bfloat16 [128, 64, 2048], P(None, None, 'grp'), may hold values from -0.75 to 0.75
- adapter_index_rows: int32 [256, 1], replicated, may hold values from 0 to 127
- queries: bfloat16 [256, 8192], P('req')
- key_value_pages: bfloat16 [10240, 16, 2, 8, 128], P('req', 'grp')
- lengths: int32 [256], P('req'), may hold values from 0 to 511, as said below
- page_slot_table: int32 [256, 32], P('req'), may hold values from 0 to 255, as said below
- departing_slots: int32 [1024], P('req'), may hold values from 0 to 255, as said below
- departing_target: int32 [1024, 1], P('req'), may hold values from 0 to 31; in each aligned block of 32 rows (0 to 31, 32 to 63, ...) at most 2 rows name the same one
Outputs:
- attention: bfloat16 [256, 8192], P('req')
- migrated_pool: bfloat16 [10240, 16, 2, 8, 128], P('req', 'grp')
Inputs may be any that keep to these rules, and one draw needn't show every extreme that they name: `adapter_index_rows`: each row names one adapter; every adapter is named by some request. `lengths`: some request has an empty cache and some has 511 cached tokens. `page_slot_table`: the rows of the requests of one home together name each of that home's slots 0 .. 255 exactly once. `departing_slots`: the 32 entries of one home are distinct. `departing_target`: the 32 rows of one home name one target at most 2 times; some home names some target exactly 2 times.
All inputs are finite; a program needn't handle non-finite values.
Results may differ from a plain program's by a relative error of at most 0.01345.
Values may be sent and summed in bfloat16 or wider, within the bound.
No kernel may reach another device: no remote copies, remote signals or barrier semaphores. Data moves between devices by JAX's collectives and lax.ppermute only.
A program may use at most 64 MiB of HBM per device.

v0:
```python
import math
import jax
import jax.numpy as jnp
from jax import lax
from jax.sharding import PartitionSpec as P

adapter_scale = 2.0
masked_score = -1e30


def merged_2(part, axis, combine):
    gathered = jax.tree.map(lambda a: lax.all_gather(a, axis), part)

    def take(source):
        return jax.tree.map(lambda a: lax.dynamic_index_in_dim(a, source, 0, False), gathered)

    return lax.fori_loop(
        1, lax.axis_size(axis), lambda source, state: combine(state, take(source)), take(0)
    )


def softmax_join(first, second):
    top = jnp.maximum(first[0], second[0])
    scale_one = jnp.exp(first[0] - top)
    scale_two = jnp.exp(second[0] - top)
    return (
        top,
        first[1] * scale_one + second[1] * scale_two,
        first[2] * scale_one[..., None] + second[2] * scale_two[..., None],
    )


def project_sums(base_part, mid_part):
    return (
        lax.psum_scatter(base_part, "req", scatter_dimension=0, tiled=True),
        lax.psum_scatter(mid_part, "req", scatter_dimension=0, tiled=True),
    )


def shards(
    normed_token_input,
    key_value_weight,
    adapter_down_weight,
    adapter_up_weight,
    adapter_index_rows,
    queries,
    key_value_pages,
    lengths,
    page_slot_table,
    departing_slots,
    departing_target,
):
    selected_adapter = adapter_index_rows[:, 0]
    rank_span_width = adapter_down_weight.shape[2]
    base_part = jnp.dot(normed_token_input, key_value_weight, preferred_element_type=jnp.float32)
    rank_portion = lax.all_gather(adapter_down_weight, "grp", axis=1, tiled=True)
    count = rank_portion.shape[1]
    flat = rank_portion.reshape(rank_portion.shape[0], count * rank_span_width)
    products = jnp.dot(normed_token_input, flat, preferred_element_type=jnp.float32).reshape(
        -1, count, rank_span_width
    )
    picker = (selected_adapter[:, None] == jnp.arange(count, dtype=jnp.int32)[None, :]).astype(
        jnp.float32
    )
    mid_part = jnp.einsum("ia,iaw->iw", picker, products)
    base_resident, mid_home = project_sums(base_part, mid_part)
    rows = lengths.shape[0]
    slot_tokens = key_value_pages.shape[1]
    heads = key_value_pages.shape[3]
    head_dim = key_value_pages.shape[4]
    group_index = lax.axis_index("grp")
    page_size = slot_tokens * lax.axis_size("grp")
    key_width = heads * head_dim
    resident_adapters = lax.dynamic_slice_in_dim(
        selected_adapter, lax.axis_index("req") * rows, rows
    )
    rank_half = adapter_up_weight.shape[1]
    column_span = adapter_up_weight.shape[2]
    mid_cast = mid_home.astype(jnp.bfloat16)
    is_value = group_index * column_span >= key_width
    mid_used = jnp.where(is_value, mid_cast[:, rank_half:], mid_cast[:, :rank_half])
    up_weight_rows = adapter_up_weight[resident_adapters]
    adapter_update = jnp.einsum(
        "ir,irc->ic", mid_used, up_weight_rows, preferred_element_type=jnp.float32
    )
    fresh_columns = (base_resident + adapter_scale * adapter_update).astype(jnp.bfloat16)
    new_all = lax.all_gather(fresh_columns, "grp", axis=1, tiled=True)
    new_keys = new_all[:, :key_width].reshape(rows, heads, head_dim)
    new_values = new_all[:, key_width:].reshape(rows, heads, head_dim)
    request_index = jnp.arange(rows, dtype=jnp.int32)
    page_slot = page_slot_table[request_index, lengths // page_size]
    offset = lengths % page_size
    mine = offset // slot_tokens == group_index
    token_local = offset % slot_tokens
    current = key_value_pages[page_slot, token_local]
    fresh = jnp.stack([new_keys, new_values], axis=1)
    written = key_value_pages.at[page_slot, token_local].set(
        jnp.where(mine[:, None, None, None], fresh, current)
    )
    pages = page_slot_table.shape[1]
    gathered = written[page_slot_table]
    keys = gathered[:, :, :, 0].reshape(rows, pages * slot_tokens, heads, head_dim)
    values = gathered[:, :, :, 1].reshape(rows, pages * slot_tokens, heads, head_dim)
    query = queries.reshape(rows, heads, -1, head_dim)
    scores = jnp.einsum(
        "ihgd,inhd->ihgn", query, keys, preferred_element_type=jnp.float32
    ) / math.sqrt(head_dim)
    positions = (
        jnp.arange(pages, dtype=jnp.int32)[:, None] * page_size
        + group_index * slot_tokens
        + jnp.arange(slot_tokens, dtype=jnp.int32)[None, :]
    ).reshape(-1)
    valid = (positions[None, :] <= lengths[:, None])[:, None, None, :]
    scores = jnp.where(valid, scores, masked_score)
    local_top = jnp.max(scores, axis=3)
    weights = jnp.where(valid, jnp.exp(scores - local_top[..., None]), 0.0)
    local_total = jnp.sum(weights, axis=3)
    local_mixed = jnp.einsum("ihgn,inhd->ihgd", weights, values, preferred_element_type=jnp.float32)
    merged = merged_2((local_top, local_total, local_mixed), "grp", softmax_join)
    total = merged[1]
    mixed = merged[2]
    attention = (mixed / total[..., None]).astype(jnp.bfloat16).reshape(rows, -1)
    targets = departing_target[:, 0]
    count_out = departing_slots.shape[0]
    order = jnp.arange(count_out, dtype=jnp.int32)
    earlier = (targets[:, None] == targets[None, :]) & (order[None, :] < order[:, None])
    place = jnp.sum(earlier.astype(jnp.int32), axis=1)
    live_slots = rows * pages
    home_count = lax.axis_size("req")
    capacity = (key_value_pages.shape[0] - live_slots) // home_count
    outbound = (
        jnp.zeros((home_count, capacity) + key_value_pages.shape[1:], key_value_pages.dtype)
        .at[targets, place]
        .set(written[departing_slots])
    )
    arrived = lax.all_to_all(outbound, "req", split_axis=0, concat_axis=0, tiled=True)
    migrated_pool = jnp.concatenate(
        [
            written[:live_slots],
            arrived.reshape((home_count * capacity,) + key_value_pages.shape[1:]),
        ],
        axis=0,
    )
    return (attention, migrated_pool)


def solution(mesh):
    in_specs = (
        P(None, "req"),
        P("req", "grp"),
        P("req", "grp", None),
        P(None, None, "grp"),
        P(),
        P("req", None),
        P("req", "grp", None, None, None),
        P("req"),
        P("req", None),
        P("req"),
        P("req", None),
    )
    out_specs = (P("req", None), P("req", "grp", None, None, None))
    return jax.shard_map(shards, mesh=mesh, in_specs=in_specs, out_specs=out_specs, check_vma=False)
```

profile of v0, /device:TPU:2, one launch (start us, length us, event | category | flops | bytes accessed | tf_op | source)
XLA Modules:
  0.0 464.8 jit_solution(6286880363566124155)
XLA Ops:
  8.1 1.5 copy.81
  9.6 1.7 fusion.37
  13.2 1.1 gather_fusion
  14.4 1.2 shift-left_bitcast_fusion
  18.2 1.4 fusion.17
  19.6 1.3 dynamic-slice.1
  21.5 1.3 gather_fusion.1
  22.9 1.2 gather_fusion.2
  24.0 120.0 %all-gather.6.cloned.1.call-done = bf16[256,128,128]{2,1,0:T(8,128)(2,1)} async-done(((bf16[256,8,128]{2,1,0:T(8,128)(2,1)}), bf16[256,128,128]{2,1,0:T(8,128)(2,1)}) %all-gather.6.cloned.1.call-update) | async-done | bytes 8388624 | tf_op jit(solution)/shard_map/all_gather | solution.py:56
  144.0 12.8 %copy.40 = bf16[256,128,128]{0,2,1:T(8,128)(2,1)} copy(bf16[256,128,128]{2,1,0:T(8,128)(2,1)} %all-gather.6.cloned.1.call-done) | data formatting | bytes 16777216 | tf_op jit(solution)/shard_map/reshape | solution.py:58
  156.8 11.1 %fusion.5 = bf16[256,128,128]{2,0,1:T(8,128)(2,1)} fusion(bf16[256,128,128]{0,2,1:T(8,128)(2,1)} %copy.40, bf16[256,256]{1,0:T(8,128)(2,1)S(1)} %copy-done.5), kind=kOutput, calls=%fused_computation.17 | convolution fusion | flops 2147483648 | bytes 16908288 | tf_op jit(solution)/shard_map/dot_general | solution.py:59
  167.9 11.1 %fusion.3 = f32[256,1,128]{2,1,0:T(1,128)} fusion(bf16[256,128,128]{2,0,1:T(8,128)(2,1)} %fusion.5, pred[256,128,1]{1,0,2:T(32,128)(4,1)S(1)} %copy-done.8), kind=kOutput, calls=%fused_computation.15 | convolution fusion | flops 8388608 | bytes 8552448 | tf_op jit(solution)/shard_map/ia,iaw->iw/dot_general | solution.py:65
  179.1 119.3 %all-reduce.7 = bf16[256,128]{1,0:T(8,128)(2,1)S(1)} all-reduce(f32[256,128]{1,0:T(8,128)} %bitcast.109), channel_id=6, replica_groups=mesh['req'=32,'grp'=16] {'req'}, use_global_device_ids=true, to_apply=%region_1.0.clone | all-reduce | flops 32768 | bytes 196608
  298.4 1.0 fusion.21
  300.1 28.9 %all_gather.25 = bf16[8,2048]{1,0:T(8,128)(2,1)S(1)} all-gather(bf16[8,128]{1,0:T(8,128)(2,1)S(1)} %fusion.20), channel_id=1, replica_groups=mesh['req'=32,'grp'=16] {'grp'}, dimensions={1}, use_global_device_ids=true | all-gather | bytes 34816 | tf_op jit(solution)/shard_map/all_gather | solution.py:87
  329.2 0.8 scatter_fusion
  330.1 1.8 gather_fusion.3
  331.8 1.3 fusion.35
  334.3 1.0 fusion.9
  335.4 0.9 convert_reduce_fusion
  338.3 3.6 scatter_fusion.1
  341.8 9.8 %all-to-all-start = ((bf16[32,2,1,2,8,128]{5,4,3,1,2,0:T(8,128)(2,1)}), bf16[32,2,1,2,8,128]{5,4,3,1,2,0:T(8,128)(2,1)}, u32[]{:S(2)}, u32[]{:S(2)}) async-start(bf16[32,2,1,2,8,128]{5,4,3,1,2,0:T(8,128)(2,1)} %bitcast.105), calls=%async_computation | async-start | bytes 524288 | tf_op jit(solution)/shard_map/all_to_all | solution.py:136
  351.6 33.6 %all-gather = f32[128,8,8]{2,1,0:T(8,128)S(1)} all-gather(f32[8,8,8]{2,1,0:T(8,128)} %copy-done.6), channel_id=2, replica_groups=mesh['req'=32,'grp'=16] {'grp'}, dimensions={0}, use_global_device_ids=true | all-gather | bytes 34816 | tf_op jit(solution)/shard_map/all_gather | solution.py:12
  385.2 1.4 fusion.11
  386.6 33.6 %all-gather.1 = f32[128,8,8]{2,1,0:T(8,128)S(1)} all-gather(f32[8,8,8]{2,1,0:T(8,128)S(1)} %fusion.11), channel_id=3, replica_groups=mesh['req'=32,'grp'=16] {'grp'}, dimensions={0}, use_global_device_ids=true | all-gather | bytes 34816 | tf_op jit(solution)/shard_map/all_gather | solution.py:12
  421.0 1.1 slice_bitcast_fusion
  422.2 2.5 pad_maximum_fusion
  424.7 1.0 slice.57
  425.6 30.8 %while.19 = (s32[]{:T(128)}, f32[8,8,8]{2,1,0:T(8,128)S(1)}, f32[8,8,8]{2,1,0:T(8,128)S(1)}, f32[8,8,8,128]{3,2,1,0:T(8,128)S(1)}, f32[16,8,8,8]{3,2,1,0:T(8,128...) while((s32[]{:T(128)}, f32[8,8,8]{2,1,0:T(8,128)S(1)}, ...), condition=%wide.region_6.7_spmd, body=%wide.region_5.6_spmd.sunk | while | flops 199685 | bytes 807055 | solution.py:17
  425.7 0.8 fusion.43
  426.5 1.2 fusion.44
  427.7 0.8 fusion.43
  428.5 1.2 fusion.44
  429.8 0.8 fusion.43
  430.6 1.2 fusion.44
  432.7 1.2 fusion.44
  433.9 0.8 fusion.43
  434.7 1.2 fusion.44
  436.8 1.2 fusion.44
  438.8 1.2 fusion.44
  440.9 1.2 fusion.44
  442.9 1.2 fusion.44
  445.0 1.2 fusion.44
  447.0 1.2 fusion.44
  449.1 1.2 fusion.44
  451.2 1.2 fusion.44
  453.2 1.2 fusion.44
  455.3 1.2 fusion.44
  (72 shorter events, 19.4 us)
Async XLA Ops:
  8.0 13.5 %copy-start = (bf16[128,64,128]{2,1,0:T(8,128)(2,1)S(1)}, bf16[128,64,128]{2,1,0:T(8,128)(2,1)}, u32[]{:S(2)}) copy-start(bf16[128,64,128]{2,1,0:T(8,128)(2,1)} %param.16) | copy-start | bytes 6291460
  8.0 1.6 copy-start.5
  8.0 3.9 copy-start.10
  8.0 5.2 %copy-start.1 = (s32[8,32]{1,0:T(8,128)S(1)}, s32[8,32]{1,0:T(8,128)}, u32[]{:S(2)}) copy-start(s32[8,32]{1,0:T(8,128)} %param.21) | copy-start | bytes 3076
  8.0 136.0 %all-gather.6.cloned.1.call-start = ((), (), s32[]{:S(2)}) async-start(), calls=%async_computation.1 | async-start | bytes 8912896 | tf_op jit(solution)/shard_map/all_gather | solution.py:56
  9.6 289.9 %all-reduce.6.cloned.1.call-start = ((), (), s32[]{:S(2)}) async-start(), calls=%async_computation.3 | async-start | bytes 262144
  11.3 413.3 %all-gather.8.cloned.1.call-start = ((), (), s32[]{:S(2)}) async-start(), calls=%async_computation.2 | async-start | bytes 4456448 | tf_op jit(solution)/shard_map/all_gather | solution.py:12
  156.8 11.1 %copy-start.8 = (pred[256,128,1]{1,0,2:T(32,128)(4,1)S(1)}, pred[256,128,1]{1,0,2:T(32,128)(4,1)}, u32[]{:S(2)}) copy-start(pred[256,128,1]{1,0,2:T(32,128)(4,1)} %fusion.17) | copy-start | bytes 98308
  167.9 161.1 %copy-start.7 = (bf16[8,2,8,128]{3,2,1,0:T(8,128)(2,1)S(1)}, bf16[8,2,8,128]{3,2,1,0:T(8,128)(2,1)}, u32[]{:S(2)}) copy-start(bf16[8,2,8,128]{3,2,1,0:T(8,128)(2,1)} %gather_fusion.2) | copy-start | bytes 98308
  167.9 161.2 %copy-start.9 = (pred[8]{0:T(512)(128)(4,1)S(1)}, pred[8]{0:T(512)(128)(4,1)}, u32[]{:S(2)}) copy-start(pred[8]{0:T(512)(128)(4,1)} %fusion.24) | copy-start | bytes 28
  330.0 3.1 copy-start.11
  331.8 3.5 copy-start.12
  333.6 0.7 copy-start.2
  333.6 0.7 copy-start.6
  341.8 80.4 %all-to-all-start = ((bf16[32,2,1,2,8,128]{5,4,3,1,2,0:T(8,128)(2,1)}), bf16[32,2,1,2,8,128]{5,4,3,1,2,0:T(8,128)(2,1)}, u32[]{:S(2)}, u32[]{:S(2)}) async-start(bf16[32,2,1,2,8,128]{5,4,3,1,2,0:T(8,128)(2,1)} %bitcast.105), calls=%async_computation | async-start | bytes 524288 | tf_op jit(solution)/shard_map/all_to_all | solution.py:136
  385.2 1.4 copy-start.3
  420.3 0.8 copy-start.4
Sparse Core Ops, SparseCore 0:
  10.9 133.1 all-gather.5
  335.4 77.9 all-gather.7
Sparse Core Ops, SparseCore 1:
  13.8 136.9 all-reduce.5
where the time goes:
time: 467 us; the launch traced here: 465 us
  blocking collectives  215 us (46%)
  waiting for transfers between devices  120 us (26%)
  other arithmetic  43.3 us (9%)
  local copies, waits for them, and re-layouts  33 us (7%)
  matrix products  26.4 us (6%)
  between operations  16.4 us (4%)
  starting transfers between devices  9.88 us (2%)
    all_gather x1, waiting for transfers between devices, shards(): lax.all_gather(adapter_down_weight, 'grp', axis=1, tiled=True)  120 us
    unnamed x1, blocking collectives  119 us
    all_gather x2, blocking collectives, merged_2(): gathered = jax.tree.map(lambda a: lax.all_gather(a, axis), part)  67.3 us
    all_gather x1, blocking collectives, shards(): new_all = lax.all_gather(fresh_columns, 'grp', axis=1, tiled=True)  28.9 us
    add x15, other arithmetic, softmax_join(): first[2] * scale_one[..., None] + second[2] * scale_two[..., None]  18.2 us
    reshape x1, local copies, waits for them, and re-layouts, shards(): flat = rank_portion.reshape(rank_portion.shape[0], count * rank_span_width)  12.8 us
    add x15, other arithmetic, softmax_join(): first[1] * scale_one + second[1] * scale_two  12.3 us
    dot_general x1, matrix products, shards(): mid_part = jnp.einsum('ia,iaw->iw', picker, products)  11.1 us
  transfers between devices with their start and end apart: 4, of which 1 were waited for; matrix products, arithmetic and copies ran while one was open for 13% of the time, Pallas kernels for 0%

commit v1 on v0

--- a/solution.py
+++ b/solution.py
@@ -53,7 +53,32 @@
     selected_adapter = adapter_index_rows[:, 0]
     rank_span_width = adapter_down_weight.shape[2]
     base_part = jnp.dot(normed_token_input, key_value_weight, preferred_element_type=jnp.float32)
-    rank_portion = lax.all_gather(adapter_down_weight, "grp", axis=1, tiled=True)
+    side_arr, carry_in, latest = (
+        lax.axis_size("grp"),
+        lax.axis_index("grp"),
+        adapter_down_weight.shape[1],
+    )
+    store = [(m, (m + 1) % side_arr) for m in range(side_arr)]
+    leaves = [(m, (m - 1) % side_arr) for m in range(side_arr)]
+    rank_portion = jnp.zeros(
+        (*adapter_down_weight.shape[:1], side_arr * latest, *adapter_down_weight.shape[1 + 1 :]),
+        adapter_down_weight.dtype,
+    )
+    rank_portion = lax.dynamic_update_slice_in_dim(
+        rank_portion, adapter_down_weight, carry_in * latest, axis=1
+    )
+    passed = block_out = adapter_down_weight
+    inter = side_arr // 2
+    for p in range(1, inter + 1):
+        passed = lax.ppermute(passed, axis_name="grp", perm=store)
+        rank_portion = lax.dynamic_update_slice_in_dim(
+            rank_portion, passed, (carry_in - p) % side_arr * latest, axis=1
+        )
+        if p < side_arr - inter:
+            block_out = lax.ppermute(block_out, axis_name="grp", perm=leaves)
+            rank_portion = lax.dynamic_update_slice_in_dim(
+                rank_portion, block_out, (carry_in + p) % side_arr * latest, axis=1
+            )
     count = rank_portion.shape[1]
     flat = rank_portion.reshape(rank_portion.shape[0], count * rank_span_width)
     products = jnp.dot(normed_token_input, flat, preferred_element_type=jnp.float32).reshape(

time: 467 us -> 473 us (1.013)
  the two profiles are of different devices: /device:TPU:2 before, /device:TPU:16 now
where the time goes in v1:
time: 473 us; the launch traced here: 470 us
  blocking collectives  199 us (42%)
  starting transfers between devices  82.3 us (17%)
  local copies, waits for them, and re-layouts  63.7 us (13%)
  other arithmetic  40.4 us (9%)
  matrix products  35.3 us (7%)
  waiting for transfers between devices  33.8 us (7%)
  between operations  15.3 us (3%)
    unnamed x1, blocking collectives  105 us
    all_gather x2, blocking collectives, merged_2(): gathered = jax.tree.map(lambda a: lax.all_gather(a, axis), part)  67.6 us
    ppermute x7, starting transfers between devices, shards(): block_out = lax.ppermute(block_out, axis_name='grp', perm=leaves)  40.7 us
    ppermute x8, waiting for transfers between devices, shards(): passed = lax.ppermute(passed, axis_name='grp', perm=store)  33.2 us
    all_gather x1, blocking collectives, shards(): new_all = lax.all_gather(fresh_columns, 'grp', axis=1, tiled=True)  26.1 us
    all_to_all x1, starting transfers between devices, shards(): lax.all_to_all(outbound, 'req', split_axis=0, concat_axis=0, tiled=True)  24.2 us
    dot_general x1, matrix products, shards(): jnp.dot(normed_token_input, flat, preferred_element_type=jnp.float32)  23.8 us
    add x15, other arithmetic, softmax_join(): first[2] * scale_one[..., None] + second[2] * scale_two[..., None]  18.2 us
  transfers between devices with their start and end apart: 18, of which 7 were waited for; matrix products, arithmetic and copies ran while one was open for 20% of the time, Pallas kernels for 0%

profile of v1, /device:TPU:16, one launch (start us, length us, event | category | flops | bytes accessed | tf_op | source)
XLA Modules:
  0.0 469.8 jit_solution(15546760080448728901)
XLA Ops:
  7.2 1.5 copy.97
  8.7 3.8 collective-permute-start
  12.5 9.5 %collective-permute-start.1 = (bf16[256,8,128]{2,1,0:T(8,128)(2,1)}, bf16[256,8,128]{2,1,0:T(8,128)(2,1)}, u32[]{:S(2)}, u32[]{:S(2)}) collective-permute-start(bf16[256,8,128]{2,1,0:T(8,128)(2,1)} %param.15), channel_id=1, source_target_pairs={{0,15},{1,0},{2,1},{3,2},{4,3},{5,4},{6,5},{7,6},{8,7},{9,8},{10,9... | collective-permute-start | bytes 1572872 | tf_op jit(solution)/shard_map/ppermute | solution.py:78
  22.0 10.3 %collective-permute-done = bf16[256,8,128]{2,1,0:T(8,128)(2,1)} collective-permute-done((bf16[256,8,128]{2,1,0:T(8,128)(2,1)}, bf16[256,8,128]{2,1,0:T(8,128)(2,1)}, u32[]{:S(2)}, u32[]{:S(2)}) %collective-permute-start) | collective-permute-done | bytes 524320 | tf_op jit(solution)/shard_map/ppermute | solution.py:73
  32.3 1.9 collective-permute-start.2
  34.3 5.1 %collective-permute-start.3 = (bf16[256,8,128]{2,1,0:T(8,128)(2,1)}, bf16[256,8,128]{2,1,0:T(8,128)(2,1)}, u32[]{:S(2)}, u32[]{:S(2)}) collective-permute-start(bf16[256,8,128]{2,1,0:T(8,128)(2,1)} %collective-permute-done.1), channel_id=1, source_target_pairs={{0,15},{1,0},{2,1},{3,2},{4,3},{5,4},{6,5},{7,6},{8,7},{9,8},{10,9... | collective-permute-start | bytes 1572872 | tf_op jit(solution)/shard_map/ppermute | solution.py:78
  39.4 1.7 fusion.36
  41.2 7.6 %collective-permute-done.2 = bf16[256,8,128]{2,1,0:T(8,128)(2,1)} collective-permute-done((bf16[256,8,128]{2,1,0:T(8,128)(2,1)}, bf16[256,8,128]{2,1,0:T(8,128)(2,1)}, u32[]{:S(2)}, u32[]{:S(2)}) %collective-permute-start.2) | collective-permute-done | bytes 524320 | tf_op jit(solution)/shard_map/ppermute | solution.py:73
  48.8 1.9 collective-permute-start.4
  51.5 5.1 %collective-permute-start.5 = (bf16[256,8,128]{2,1,0:T(8,128)(2,1)}, bf16[256,8,128]{2,1,0:T(8,128)(2,1)}, u32[]{:S(2)}, u32[]{:S(2)}) collective-permute-start(bf16[256,8,128]{2,1,0:T(8,128)(2,1)} %collective-permute-done.3), channel_id=1, source_target_pairs={{0,15},{1,0},{2,1},{3,2},{4,3},{5,4},{6,5},{7,6},{8,7},{9,8},{10,9... | collective-permute-start | bytes 1572872 | tf_op jit(solution)/shard_map/ppermute | solution.py:78
  57.3 1.3 gather_fusion
  58.6 5.8 %collective-permute-done.4 = bf16[256,8,128]{2,1,0:T(8,128)(2,1)} collective-permute-done((bf16[256,8,128]{2,1,0:T(8,128)(2,1)}, bf16[256,8,128]{2,1,0:T(8,128)(2,1)}, u32[]{:S(2)}, u32[]{:S(2)}) %collective-permute-start.4) | collective-permute-done | bytes 524320 | tf_op jit(solution)/shard_map/ppermute | solution.py:73
  64.5 1.9 collective-permute-start.6
  67.8 5.1 %collective-permute-start.7 = (bf16[256,8,128]{2,1,0:T(8,128)(2,1)}, bf16[256,8,128]{2,1,0:T(8,128)(2,1)}, u32[]{:S(2)}, u32[]{:S(2)}) collective-permute-start(bf16[256,8,128]{2,1,0:T(8,128)(2,1)} %collective-permute-done.5), channel_id=1, source_target_pairs={{0,15},{1,0},{2,1},{3,2},{4,3},{5,4},{6,5},{7,6},{8,7},{9,8},{10,9... | collective-permute-start | bytes 1572872 | tf_op jit(solution)/shard_map/ppermute | solution.py:78
  72.9 5.4 %broadcast_in_dim.69 = bf16[256,128,128]{2,1,0:T(8,128)(2,1)} broadcast(bf16[]{:T(256)} %constant.211.clone.1), dimensions={} | broadcast | bytes 8388610 | tf_op jit(solution)/shard_map/broadcast_in_dim | solution.py:63
  79.3 1.9 collective-permute-start.8
  81.9 5.6 %collective-permute-start.9 = (bf16[256,8,128]{2,1,0:T(8,128)(2,1)}, bf16[256,8,128]{2,1,0:T(8,128)(2,1)}, u32[]{:S(2)}, u32[]{:S(2)}) collective-permute-start(bf16[256,8,128]{2,1,0:T(8,128)(2,1)} %collective-permute-done.7), channel_id=1, source_target_pairs={{0,15},{1,0},{2,1},{3,2},{4,3},{5,4},{6,5},{7,6},{8,7},{9,8},{10,9... | collective-permute-start | bytes 1572872 | tf_op jit(solution)/shard_map/ppermute | solution.py:78
  87.5 5.9 %collective-permute-done.8 = bf16[256,8,128]{2,1,0:T(8,128)(2,1)} collective-permute-done((bf16[256,8,128]{2,1,0:T(8,128)(2,1)}, bf16[256,8,128]{2,1,0:T(8,128)(2,1)}, u32[]{:S(2)}, u32[]{:S(2)}) %collective-permute-start.8) | collective-permute-done | bytes 524320 | tf_op jit(solution)/shard_map/ppermute | solution.py:73
  93.4 1.9 collective-permute-start.10
  99.4 2.0 constant_dynamic-update-slice_fusion.14
  101.4 1.9 constant_dynamic-update-slice_fusion.13
  103.3 1.9 constant_dynamic-update-slice_fusion.12
  105.2 5.1 %collective-permute-start.11 = (bf16[256,8,128]{2,1,0:T(8,128)(2,1)}, bf16[256,8,128]{2,1,0:T(8,128)(2,1)S(1)}, u32[]{:S(2)}, u32[]{:S(2)}) collective-permute-start(bf16[256,8,128]{2,1,0:T(8,128)(2,1)} %collective-permute-done.9), channel_id=1, source_target_pairs={{0,15},{1,0},{2,1},{3,2},{4,3},{5,4},{6,5},{7,6},{8,7},{9,8},{10,9... | collective-permute-start | bytes 1572872 | tf_op jit(solution)/shard_map/ppermute | solution.py:78
  110.3 2.0 constant_dynamic-update-slice_fusion.11
  112.3 1.9 collective-permute-start.12
  114.2 1.9 constant_dynamic-update-slice_fusion.10
  116.1 1.9 constant_dynamic-update-slice_fusion.9
  118.1 1.9 constant_dynamic-update-slice_fusion.8
  120.0 2.0 constant_dynamic-update-slice_fusion.7
  122.0 5.1 %collective-permute-start.13 = (bf16[256,8,128]{2,1,0:T(8,128)(2,1)S(1)}, bf16[256,8,128]{2,1,0:T(8,128)(2,1)S(1)}, u32[]{:S(2)}, u32[]{:S(2)}) collective-permute-start(bf16[256,8,128]{2,1,0:T(8,128)(2,1)S(1)} %collective-permute-done.11), channel_id=1, source_target_pairs={{0,15},{1,0},{2,1},{3,2},{4,3},{5,4},{6,5},{7,6},{8,7},{9,8},{10,9... | collective-permute-start | bytes 1572872 | tf_op jit(solution)/shard_map/ppermute | solution.py:78
  127.1 2.0 constant_dynamic-update-slice_fusion.6
  129.1 2.1 collective-permute-start.14
  131.2 1.9 constant_dynamic-update-slice_fusion.5
  133.1 2.0 constant_dynamic-update-slice_fusion.4
  137.9 3.5 collective-permute-done.14
  142.3 23.8 %fusion.3 = bf16[16384,256]{1,0:T(8,128)(2,1)} fusion(bf16[256,256]{1,0:T(8,128)(2,1)S(1)} %copy-done.4, bf16[32,8,128,128]{3,2,1,0:T(8,128)(2,1)} %bitcast.39), kind=kOutput, calls=%fused_computation.15 | convolution fusion | flops 2147483648 | bytes 16908288 | tf_op jit(solution)/shard_map/dot_general | solution.py:84
  166.1 12.5 %copy.34 = bf16[256,128,128]{2,1,0:T(8,128)(2,1)} copy(bf16[256,128,128]{0,2,1:T(8,128)(2,1)} %bitcast.100) | data formatting | bytes 16777216 | tf_op jit(solution)/shard_map/reshape | solution.py:84
  178.6 6.3 %fusion.9 = f32[256,1,128]{2,1,0:T(1,128)} fusion(bf16[256,128,128]{2,1,0:T(8,128)(2,1)} %copy.34, pred[256,128,1]{1,0,2:T(32,128)(4,1)S(1)} %fusion.16), kind=kOutput, calls=%fused_computation.26 | convolution fusion | flops 8388608 | bytes 8552448 | tf_op jit(solution)/shard_map/ia,iaw->iw/dot_general | solution.py:90
  184.9 105.0 %all-reduce.7 = bf16[256,128]{1,0:T(8,128)(2,1)S(1)} all-reduce(f32[256,128]{1,0:T(8,128)} %bitcast.107), channel_id=6, replica_groups=mesh['req'=32,'grp'=16] {'req'}, use_global_device_ids=true, to_apply=%region_1.2.clone | all-reduce | flops 32768 | bytes 196608
  291.7 26.1 %all_gather.21 = bf16[8,2048]{1,0:T(8,128)(2,1)S(1)} all-gather(bf16[8,128]{1,0:T(8,128)(2,1)S(1)} %fusion.19), channel_id=1, replica_groups=mesh['req'=32,'grp'=16] {'grp'}, dimensions={1}, use_global_device_ids=true | all-gather | bytes 34816 | tf_op jit(solution)/shard_map/all_gather | solution.py:112
  318.7 1.8 gather_fusion.3
  321.7 1.4 fusion.35
  328.4 3.6 scatter_fusion.1
  332.0 24.2 %all-to-all-start = ((bf16[32,2,1,2,8,128]{5,4,3,1,2,0:T(8,128)(2,1)}), bf16[32,2,1,2,8,128]{5,4,3,1,2,0:T(8,128)(2,1)}, u32[]{:S(2)}, u32[]{:S(2)}) async-start(bf16[32,2,1,2,8,128]{5,4,3,1,2,0:T(8,128)(2,1)} %bitcast.103), calls=%async_computation | async-start | bytes 524288 | tf_op jit(solution)/shard_map/all_to_all | solution.py:161
  357.4 35.9 %all-gather.1 = f32[128,8,8]{2,1,0:T(8,128)S(1)} all-gather(f32[8,8,8]{2,1,0:T(8,128)S(1)} %fusion.11), channel_id=3, replica_groups=mesh['req'=32,'grp'=16] {'grp'}, dimensions={0}, use_global_device_ids=true | all-gather | bytes 34816 | tf_op jit(solution)/shard_map/all_gather | solution.py:12
  394.1 31.7 %all-gather = f32[128,8,8]{2,1,0:T(8,128)S(1)} all-gather(f32[8,8,8]{2,1,0:T(8,128)} %copy-done.6), channel_id=2, replica_groups=mesh['req'=32,'grp'=16] {'grp'}, dimensions={0}, use_global_device_ids=true | all-gather | bytes 34816 | tf_op jit(solution)/shard_map/all_gather | solution.py:12
  427.8 2.5 pad_maximum_fusion
  431.3 30.8 %while.19 = (s32[]{:T(128)}, f32[8,8,8]{2,1,0:T(8,128)S(1)}, f32[8,8,8]{2,1,0:T(8,128)S(1)}, f32[8,8,8,128]{3,2,1,0:T(8,128)S(1)}, f32[16,8,8,8]{3,2,1,0:T(8,128...) while((s32[]{:T(128)}, f32[8,8,8]{2,1,0:T(8,128)S(1)}, ...), condition=%wide.region_6.7_spmd, body=%wide.region_5.6_spmd.sunk | while | flops 199685 | bytes 807063 | solution.py:17
  (107 shorter events, 57.0 us)
Async XLA Ops:
  7.2 90.4 %copy-start = (bf16[128,64,128]{2,1,0:T(8,128)(2,1)S(1)}, bf16[128,64,128]{2,1,0:T(8,128)(2,1)}, u32[]{:S(2)}) copy-start(bf16[128,64,128]{2,1,0:T(8,128)(2,1)} %param.16) | copy-start | bytes 6291460
  7.2 74.0 %copy-start.7 = (s32[256,1]{0,1:T(1,128)S(1)}, s32[256,1]{0,1:T(1,128)}, u32[]{:S(2)}) copy-start(s32[256,1]{0,1:T(1,128)} %param.17) | copy-start | bytes 3076
  7.2 74.0 %copy-start.8 = (s32[8]{0:T(128)S(1)}, s32[8]{0:T(128)}, u32[]{:S(2)}) copy-start(s32[8]{0:T(128)} %param.20) | copy-start | bytes 100
  7.2 283.8 %all-reduce.6.cloned.1.call-start = ((), (), s32[]{:S(2)}) async-start(), calls=%async_computation.2 | async-start | bytes 262144
  8.7 23.6 %collective-permute-start = (bf16[256,8,128]{2,1,0:T(8,128)(2,1)}, bf16[256,8,128]{2,1,0:T(8,128)(2,1)}, u32[]{:S(2)}, u32[]{:S(2)}) collective-permute-start(bf16[256,8,128]{2,1,0:T(8,128)(2,1)} %param.15), channel_id=1, source_target_pairs={{0,1},{1,2},{2,3},{3,4},{4,5},{5,6},{6,7},{7,8},{8,9},{9,10},{10,1... | collective-permute-start | bytes 1572872 | tf_op jit(solution)/shard_map/ppermute | solution.py:73
  12.5 21.7 %collective-permute-start.1 = (bf16[256,8,128]{2,1,0:T(8,128)(2,1)}, bf16[256,8,128]{2,1,0:T(8,128)(2,1)}, u32[]{:S(2)}, u32[]{:S(2)}) collective-permute-start(bf16[256,8,128]{2,1,0:T(8,128)(2,1)} %param.15), channel_id=1, source_target_pairs={{0,15},{1,0},{2,1},{3,2},{4,3},{5,4},{6,5},{7,6},{8,7},{9,8},{10,9... | collective-permute-start | bytes 1572872 | tf_op jit(solution)/shard_map/ppermute | solution.py:78
  32.3 16.5 %collective-permute-start.2 = (bf16[256,8,128]{2,1,0:T(8,128)(2,1)}, bf16[256,8,128]{2,1,0:T(8,128)(2,1)}, u32[]{:S(2)}, u32[]{:S(2)}) collective-permute-start(bf16[256,8,128]{2,1,0:T(8,128)(2,1)} %collective-permute-done), channel_id=1, source_target_pairs={{0,1},{1,2},{2,3},{3,4},{4,5},{5,6},{6,7},{7,8},{8,9},{9,10},{10,1... | collective-permute-start | bytes 1572872 | tf_op jit(solution)/shard_map/ppermute | solution.py:73
  34.3 17.2 %collective-permute-start.3 = (bf16[256,8,128]{2,1,0:T(8,128)(2,1)}, bf16[256,8,128]{2,1,0:T(8,128)(2,1)}, u32[]{:S(2)}, u32[]{:S(2)}) collective-permute-start(bf16[256,8,128]{2,1,0:T(8,128)(2,1)} %collective-permute-done.1), channel_id=1, source_target_pairs={{0,15},{1,0},{2,1},{3,2},{4,3},{5,4},{6,5},{7,6},{8,7},{9,8},{10,9... | collective-permute-start | bytes 1572872 | tf_op jit(solution)/shard_map/ppermute | solution.py:78
  41.2 389.2 %all-gather.5.cloned.1.call-start = ((), (), s32[]{:S(2)}) async-start(), calls=%async_computation.1 | async-start | bytes 4456448 | tf_op jit(solution)/shard_map/all_gather | solution.py:12
  48.8 15.6 %collective-permute-start.4 = (bf16[256,8,128]{2,1,0:T(8,128)(2,1)}, bf16[256,8,128]{2,1,0:T(8,128)(2,1)}, u32[]{:S(2)}, u32[]{:S(2)}) collective-permute-start(bf16[256,8,128]{2,1,0:T(8,128)(2,1)} %collective-permute-done.2), channel_id=1, source_target_pairs={{0,1},{1,2},{2,3},{3,4},{4,5},{5,6},{6,7},{7,8},{8,9},{9,10},{10,1... | collective-permute-start | bytes 1572872 | tf_op jit(solution)/shard_map/ppermute | solution.py:73
  51.5 16.3 %collective-permute-start.5 = (bf16[256,8,128]{2,1,0:T(8,128)(2,1)}, bf16[256,8,128]{2,1,0:T(8,128)(2,1)}, u32[]{:S(2)}, u32[]{:S(2)}) collective-permute-start(bf16[256,8,128]{2,1,0:T(8,128)(2,1)} %collective-permute-done.3), channel_id=1, source_target_pairs={{0,15},{1,0},{2,1},{3,2},{4,3},{5,4},{6,5},{7,6},{8,7},{9,8},{10,9... | collective-permute-start | bytes 1572872 | tf_op jit(solution)/shard_map/ppermute | solution.py:78
  58.6 19.7 %copy-start.5 = (bf16[256,8,128]{2,1,0:T(8,128)(2,1)S(1)}, bf16[256,8,128]{2,1,0:T(8,128)(2,1)}, u32[]{:S(2)}) copy-start(bf16[256,8,128]{2,1,0:T(8,128)(2,1)} %param.15) | copy-start | bytes 1572868
  64.5 14.8 %collective-permute-start.6 = (bf16[256,8,128]{2,1,0:T(8,128)(2,1)}, bf16[256,8,128]{2,1,0:T(8,128)(2,1)}, u32[]{:S(2)}, u32[]{:S(2)}) collective-permute-start(bf16[256,8,128]{2,1,0:T(8,128)(2,1)} %collective-permute-done.4), channel_id=1, source_target_pairs={{0,1},{1,2},{2,3},{3,4},{4,5},{5,6},{6,7},{7,8},{8,9},{9,10},{10,1... | collective-permute-start | bytes 1572872 | tf_op jit(solution)/shard_map/ppermute | solution.py:73
  67.8 14.0 %collective-permute-start.7 = (bf16[256,8,128]{2,1,0:T(8,128)(2,1)}, bf16[256,8,128]{2,1,0:T(8,128)(2,1)}, u32[]{:S(2)}, u32[]{:S(2)}) collective-permute-start(bf16[256,8,128]{2,1,0:T(8,128)(2,1)} %collective-permute-done.5), channel_id=1, source_target_pairs={{0,15},{1,0},{2,1},{3,2},{4,3},{5,4},{6,5},{7,6},{8,7},{9,8},{10,9... | collective-permute-start | bytes 1572872 | tf_op jit(solution)/shard_map/ppermute | solution.py:78
  79.3 14.2 %collective-permute-start.8 = (bf16[256,8,128]{2,1,0:T(8,128)(2,1)}, bf16[256,8,128]{2,1,0:T(8,128)(2,1)}, u32[]{:S(2)}, u32[]{:S(2)}) collective-permute-start(bf16[256,8,128]{2,1,0:T(8,128)(2,1)} %collective-permute-done.6), channel_id=1, source_target_pairs={{0,1},{1,2},{2,3},{3,4},{4,5},{5,6},{6,7},{7,8},{8,9},{9,10},{10,1... | collective-permute-start | bytes 1572872 | tf_op jit(solution)/shard_map/ppermute | solution.py:73
  81.9 23.3 %collective-permute-start.9 = (bf16[256,8,128]{2,1,0:T(8,128)(2,1)}, bf16[256,8,128]{2,1,0:T(8,128)(2,1)}, u32[]{:S(2)}, u32[]{:S(2)}) collective-permute-start(bf16[256,8,128]{2,1,0:T(8,128)(2,1)} %collective-permute-done.7), channel_id=1, source_target_pairs={{0,15},{1,0},{2,1},{3,2},{4,3},{5,4},{6,5},{7,6},{8,7},{9,8},{10,9... | collective-permute-start | bytes 1572872 | tf_op jit(solution)/shard_map/ppermute | solution.py:78
  93.4 18.9 %collective-permute-start.10 = (bf16[256,8,128]{2,1,0:T(8,128)(2,1)}, bf16[256,8,128]{2,1,0:T(8,128)(2,1)}, u32[]{:S(2)}, u32[]{:S(2)}) collective-permute-start(bf16[256,8,128]{2,1,0:T(8,128)(2,1)} %collective-permute-done.8), channel_id=1, source_target_pairs={{0,1},{1,2},{2,3},{3,4},{4,5},{5,6},{6,7},{7,8},{8,9},{9,10},{10,1... | collective-permute-start | bytes 1572872 | tf_op jit(solution)/shard_map/ppermute | solution.py:73
  99.4 42.9 %copy-start.4 = (bf16[256,256]{1,0:T(8,128)(2,1)S(1)}, bf16[256,256]{1,0:T(8,128)(2,1)}, u32[]{:S(2)}) copy-start(bf16[256,256]{1,0:T(8,128)(2,1)} %param.13) | copy-start | bytes 393220
  105.2 16.8 %collective-permute-start.11 = (bf16[256,8,128]{2,1,0:T(8,128)(2,1)}, bf16[256,8,128]{2,1,0:T(8,128)(2,1)S(1)}, u32[]{:S(2)}, u32[]{:S(2)}) collective-permute-start(bf16[256,8,128]{2,1,0:T(8,128)(2,1)} %collective-permute-done.9), channel_id=1, source_target_pairs={{0,15},{1,0},{2,1},{3,2},{4,3},{5,4},{6,5},{7,6},{8,7},{9,8},{10,9... | collective-permute-start | bytes 1572872 | tf_op jit(solution)/shard_map/ppermute | solution.py:78
  112.3 16.8 %collective-permute-start.12 = (bf16[256,8,128]{2,1,0:T(8,128)(2,1)}, bf16[256,8,128]{2,1,0:T(8,128)(2,1)S(1)}, u32[]{:S(2)}, u32[]{:S(2)}) collective-permute-start(bf16[256,8,128]{2,1,0:T(8,128)(2,1)} %collective-permute-done.10), channel_id=1, source_target_pairs={{0,1},{1,2},{2,3},{3,4},{4,5},{5,6},{6,7},{7,8},{8,9},{9,10},{10,1... | collective-permute-start | bytes 1572872 | tf_op jit(solution)/shard_map/ppermute | solution.py:73
  122.0 15.0 %collective-permute-start.13 = (bf16[256,8,128]{2,1,0:T(8,128)(2,1)S(1)}, bf16[256,8,128]{2,1,0:T(8,128)(2,1)S(1)}, u32[]{:S(2)}, u32[]{:S(2)}) collective-permute-start(bf16[256,8,128]{2,1,0:T(8,128)(2,1)S(1)} %collective-permute-done.11), channel_id=1, source_target_pairs={{0,15},{1,0},{2,1},{3,2},{4,3},{5,4},{6,5},{7,6},{8,7},{9,8},{10,9... | collective-permute-start | bytes 1572872 | tf_op jit(solution)/shard_map/ppermute | solution.py:78
  129.1 12.3 %collective-permute-start.14 = (bf16[256,8,128]{2,1,0:T(8,128)(2,1)S(1)}, bf16[256,8,128]{2,1,0:T(8,128)(2,1)S(1)}, u32[]{:S(2)}, u32[]{:S(2)}) collective-permute-start(bf16[256,8,128]{2,1,0:T(8,128)(2,1)S(1)} %collective-permute-done.12), channel_id=1, source_target_pairs={{0,1},{1,2},{2,3},{3,4},{4,5},{5,6},{6,7},{7,8},{8,9},{9,10},{10,1... | collective-permute-start | bytes 1572872 | tf_op jit(solution)/shard_map/ppermute | solution.py:73
  323.1 0.7 copy-start.1
  323.1 0.7 copy-start.6
  332.0 95.8 %all-to-all-start = ((bf16[32,2,1,2,8,128]{5,4,3,1,2,0:T(8,128)(2,1)}), bf16[32,2,1,2,8,128]{5,4,3,1,2,0:T(8,128)(2,1)}, u32[]{:S(2)}, u32[]{:S(2)}) async-start(bf16[32,2,1,2,8,128]{5,4,3,1,2,0:T(8,128)(2,1)} %bitcast.103), calls=%async_computation | async-start | bytes 524288 | tf_op jit(solution)/shard_map/all_to_all | solution.py:161
  393.3 0.8 copy-start.2
  425.8 0.8 copy-start.3
Sparse Core Ops, SparseCore 0:
  41.3 129.7 all-reduce.5
  324.9 93.3 all-gather.4
